TPU v7x, 256 devices: a whole 4x4x8 slice. The times are simulated.
256 devices in a mesh: tm: 64 (over y, z, core), state: 4 (over x).
Axes of the slice: x: 4, y: 4, z: 8, core: 2. Of those that a mesh axis runs over, the one named last changes fastest.
Arguments:
- dynamics: float32 [512, 512], P('state'), may hold values from -1 to 1
- pattern: int32 [4, 4], replicated, may hold values from 0 to 1
- initial_mean: float32 [4, 512], replicated, may hold values from -6 to 6
- observed: float32 [1024, 4], P('tm'), may hold values from -6 to 6
- obs_index: int32 [1024], P('tm'), may hold values from 0 to 511
- obs_noise: float32 [1024], P('tm'), may hold values from 0.5 to 4
Outputs:
- filtered: float32 [1024, 4, 512], P('tm', 'state')
- smoothed: float32 [1024, 4, 512], P('tm', 'state')
All inputs are finite; a program needn't handle non-finite values.
Results may differ from a plain program's by a relative error of at most 0.0003.
Values sent between devices are 32-bit elements; how exact they have to be, the bound alone decides.
No kernel may reach another device: no remote copies, remote signals or barrier semaphores. Data moves between devices by JAX's collectives and lax.ppermute only.
A program may use at most 256 MiB of HBM per device.

v0:
```python
import jax
import jax.numpy as jnp
from jax import lax
from jax.sharding import PartitionSpec as P

AXES = ("tm", "state")


def product(left, right):
    return jnp.dot(left, right, precision=lax.Precision.HIGHEST, preferred_element_type=jnp.float32)


def transposed(left, right):
    return lax.dot_general(
        left,
        right,
        (((1,), (1,)), ((), ())),
        precision=lax.Precision.HIGHEST,
        preferred_element_type=jnp.float32,
    )


def leading(left, right):
    return lax.dot_general(
        left,
        right,
        (((0,), (0,)), ((), ())),
        precision=lax.Precision.HIGHEST,
        preferred_element_type=jnp.float32,
    )


def shifted(block, distance, total):
    route = [(i, i + distance) for i in range(total) if 0 <= i + distance < total]
    return lax.ppermute(block, AXES, route)


def per_device(dynamics, pattern, initial_mean, observed, obs_index, obs_noise):
    state_width = dynamics.shape[1]
    blocks = pattern.shape[0]
    block_span = state_width // blocks
    seq_total = initial_mean.shape[0]
    members = lax.axis_size("state")
    segments = lax.axis_size("tm") * members
    member = lax.axis_index("state")
    segment = lax.axis_index(AXES)
    span = observed.shape[0] // members
    steps_total = span * segments
    present = jnp.maximum(pattern, jnp.eye(blocks, dtype=jnp.int32))
    block_mask = jnp.repeat(jnp.repeat(present, block_span, 0), block_span, 1).astype(jnp.float32)
    transition = lax.all_gather(dynamics, "state", axis=0, tiled=True) * block_mask
    first = member * span
    obs_here = lax.dynamic_slice_in_dim(observed, first, span, 0)
    index_here = lax.dynamic_slice_in_dim(obs_index, first, span, 0)
    noise_here = lax.dynamic_slice_in_dim(obs_noise, first, span, 0)
    gains = 1.0 / (1.0 + noise_here)
    state_index = jnp.arange(state_width, dtype=jnp.int32)
    hits = (state_index[None, :] == index_here[:, None]).astype(jnp.float32)
    scales = 1.0 - gains[:, None] * hits
    global_step = segment * span + jnp.arange(span, dtype=jnp.int32)
    keeps = jnp.where(global_step == steps_total - 1, 0.0, 1.0).astype(jnp.float32)
    pushes = [(gains[j] * obs_here[j])[:, None] * hits[j][None, :] for j in range(span)]
    filt_a = transition * scales[0][:, None]
    filt_b = pushes[0]
    for j in range(1, span):
        filt_a = product(transition, filt_a) * scales[j][:, None]
        filt_b = transposed(filt_b, transition) * scales[j][None, :] + pushes[j]
    last = span - 1
    smooth_q = keeps[last] * (transition.T * scales[last][:, None])
    for j in range(last - 1, -1, -1):
        smooth_q = keeps[j] * (leading(transition, smooth_q) * scales[j][:, None])
    levels = 0
    while 2 ** (levels + 1) < segments:
        levels += 1
    stored_q = []
    for level in range(levels):
        distance = 2**level
        arrived_a, arrived_b = shifted((filt_a, filt_b), distance, segments)
        arrived_q = shifted(smooth_q, -distance, segments)
        usable = segment >= distance
        new_a = product(filt_a, arrived_a)
        new_b = transposed(arrived_b, filt_a) + filt_b
        filt_a = jnp.where(usable, new_a, filt_a)
        filt_b = jnp.where(usable, new_b, filt_b)
        stored_q.append(smooth_q)
        smooth_q = jnp.where(segment + distance < segments, product(smooth_q, arrived_q), smooth_q)
    stored_q.append(smooth_q)
    top = 2**levels
    prefix = transposed(initial_mean, filt_a) + filt_b
    if top < segments:
        arrived = shifted(prefix, top, segments)
        prefix = jnp.where(segment >= top, transposed(arrived, filt_a) + filt_b, prefix)
    entry = jnp.where(segment == 0, initial_mean, shifted(prefix, 1, segments))
    filtered = []
    current = entry
    for j in range(span):
        current = transposed(current, transition) * scales[j][None, :] + pushes[j]
        filtered.append(current)
    filtered = jnp.stack(filtered)
    mapped = product(
        transposed(filtered.reshape(span * seq_total, state_width), transition), transition
    ).reshape(span, seq_total, state_width)
    gaps = filtered - keeps[:, None, None] * mapped * scales[:, None, :]
    offsets = jnp.zeros((seq_total, state_width), jnp.float32)
    for j in range(last, -1, -1):
        offsets = keeps[j] * product(offsets, transition) * scales[j][None, :] + gaps[j]
    for level in range(levels):
        distance = 2**level
        arrived = shifted(offsets, -distance, segments)
        offsets = jnp.where(
            segment + distance < segments, transposed(arrived, stored_q[level]) + offsets, offsets
        )
    if top < segments:
        arrived = shifted(offsets, -top, segments)
        offsets = jnp.where(
            segment + top < segments, transposed(arrived, stored_q[levels]) + offsets, offsets
        )
    current = shifted(offsets, -1, segments)
    smoothed = [None] * span
    for j in range(last, -1, -1):
        current = keeps[j] * product(current, transition) * scales[j][None, :] + gaps[j]
        smoothed[j] = current
    smoothed = jnp.stack(smoothed)
    both = jnp.stack([filtered, smoothed])
    both = lax.all_to_all(both, "state", split_axis=2, concat_axis=1, tiled=True)
    return (both[0], both[1])


def solution(mesh):
    return jax.shard_map(
        per_device,
        mesh=mesh,
        in_specs=(P("state", None), P(), P(), P("tm", None), P("tm"), P("tm")),
        out_specs=(P("tm", "state", None), P("tm", "state", None)),
        check_vma=False,
    )
```

profile of v0, /device:TPU:232, one launch (start us, length us, event | category | flops | bytes accessed | tf_op | source)
XLA Modules:
  0.0 522.6 jit_solution(9289157682158466495)
XLA Ops:
  9.4 27.4 %all-gather.2.cloned.1.call-done = f32[512,512]{1,0:T(8,128)} async-done(((f32[128,512]{1,0:T(8,128)}), f32[512,512]{1,0:T(8,128)}) %all-gather.2.cloned.1.call-update) | async-done | bytes 1048592 | tf_op jit(solution)/shard_map/all_gather | solution.py:51
  46.2 20.8 %collective-permute-done = f32[512,512]{1,0:T(8,128)} collective-permute-done((f32[512,512]{1,0:T(8,128)S(1)}, f32[512,512]{1,0:T(8,128)}, u32[]{:S(2)}, u32[]{:S(2)}) %collective-permute-start) | collective-permute-done | bytes 1048608 | tf_op jit(solution)/shard_map/ppermute | solution.py:35
  70.1 6.3 %collective-permute-start.1 = (f32[512,512]{1,0:T(8,128)S(1)}, f32[512,512]{1,0:T(8,128)}, u32[]{:S(2)}, u32[]{:S(2)}) collective-permute-start(f32[512,512]{1,0:T(8,128)S(1)} %convolution_select_fusion.13), channel_id=1, source_target_pairs={{0,2},{1,3},{2,4},{3,5},{4,6},{5,7},{6,8},{7,9},{8,10},{9,11},{10,... | collective-permute-start | bytes 3145736 | tf_op jit(solution)/shard_map/ppermute | solution.py:35
  77.1 22.1 %collective-permute-done.1 = f32[512,512]{1,0:T(8,128)} collective-permute-done((f32[512,512]{1,0:T(8,128)S(1)}, f32[512,512]{1,0:T(8,128)}, u32[]{:S(2)}, u32[]{:S(2)}) %collective-permute-start.1) | collective-permute-done | bytes 1048608 | tf_op jit(solution)/shard_map/ppermute | solution.py:35
  105.0 4.9 fusion.7
  121.8 4.9 collective-permute-start.3
  129.5 13.0 %collective-permute-done.18 = f32[512,512]{1,0:T(8,128)} collective-permute-done((f32[512,512]{1,0:T(8,128)S(1)}, f32[512,512]{1,0:T(8,128)}, u32[]{:S(2)}, u32[]{:S(2)}) %collective-permute-start.18) | collective-permute-done | bytes 1048608 | tf_op jit(solution)/shard_map/ppermute | solution.py:35
  145.5 6.5 %collective-permute-start.20 = (f32[512,512]{1,0:T(8,128)S(1)}, f32[512,512]{1,0:T(8,128)S(1)}, u32[]{:S(2)}, u32[]{:S(2)}) collective-permute-start(f32[512,512]{1,0:T(8,128)S(1)} %convolution_select_fusion.6), channel_id=1, source_target_pairs={{2,0},{3,1},{4,2},{5,3},{6,4},{7,5},{8,6},{9,7},{10,8},{11,9},{12,... | collective-permute-start | bytes 3145736 | tf_op jit(solution)/shard_map/ppermute | solution.py:35
  164.1 11.0 %collective-permute-done.20 = f32[512,512]{1,0:T(8,128)S(1)} collective-permute-done((f32[512,512]{1,0:T(8,128)S(1)}, f32[512,512]{1,0:T(8,128)S(1)}, u32[]{:S(2)}, u32[]{:S(2)}) %collective-permute-start.20) | collective-permute-done | bytes 1048608 | tf_op jit(solution)/shard_map/ppermute | solution.py:35
  180.3 21.0 %collective-permute-done.7 = f32[4,512]{1,0:T(4,128)S(1)} collective-permute-done((f32[4,512]{1,0:T(4,128)S(1)}, f32[4,512]{1,0:T(4,128)S(1)}, u32[]{:S(2)}, u32[]{:S(2)}) %collective-permute-start.7) | collective-permute-done | bytes 8224 | tf_op jit(solution)/shard_map/ppermute | solution.py:35
  210.0 9.3 %collective-permute-start.5 = (f32[512,512]{1,0:T(8,128)}, f32[512,512]{1,0:T(8,128)}, u32[]{:S(2)}, u32[]{:S(2)}) collective-permute-start(f32[512,512]{1,0:T(8,128)} %convolution_select_fusion.9), channel_id=1, source_target_pairs={{0,32},{1,33},{2,34},{3,35},{4,36},{5,37},{6,38},{7,39},{8,40},{9,... | collective-permute-start | bytes 3145736 | tf_op jit(solution)/shard_map/ppermute | solution.py:35
  222.3 11.1 %collective-permute-done.9 = f32[4,512]{1,0:T(4,128)S(1)} collective-permute-done((f32[4,512]{1,0:T(4,128)S(1)}, f32[4,512]{1,0:T(4,128)S(1)}, u32[]{:S(2)}, u32[]{:S(2)}) %collective-permute-start.9) | collective-permute-done | bytes 8224 | tf_op jit(solution)/shard_map/ppermute | solution.py:35
  237.7 4.7 convolution_select_fusion.4
  246.3 14.5 %collective-permute-done.10 = f32[4,512]{1,0:T(4,128)S(1)} collective-permute-done((f32[4,512]{1,0:T(4,128)S(1)}, f32[4,512]{1,0:T(4,128)S(1)}, u32[]{:S(2)}, u32[]{:S(2)}) %collective-permute-start.10) | collective-permute-done | bytes 8224 | tf_op jit(solution)/shard_map/ppermute | solution.py:35
  263.0 18.0 %collective-permute-start.11 = (f32[4,512]{1,0:T(4,128)S(1)}, f32[4,512]{1,0:T(4,128)S(1)}, u32[]{:S(2)}, u32[]{:S(2)}) collective-permute-start(f32[4,512]{1,0:T(4,128)S(1)} %fusion.42), channel_id=1, source_target_pairs={{0,16},{1,17},{2,18},{3,19},{4,20},{5,21},{6,22},{7,23},{8,24},{9,... | collective-permute-start | bytes 24584 | tf_op jit(solution)/shard_map/ppermute | solution.py:35
  291.1 6.9 %collective-permute-done.12 = f32[4,512]{1,0:T(4,128)S(1)} collective-permute-done((f32[4,512]{1,0:T(4,128)S(1)}, f32[4,512]{1,0:T(4,128)S(1)}, u32[]{:S(2)}, u32[]{:S(2)}) %collective-permute-start.12) | collective-permute-done | bytes 8224 | tf_op jit(solution)/shard_map/ppermute | solution.py:35
  306.8 4.8 collective-permute-start.26
  328.8 30.4 %collective-permute-done.26 = f32[512,512]{1,0:T(8,128)} collective-permute-done((f32[512,512]{1,0:T(8,128)}, f32[512,512]{1,0:T(8,128)}, u32[]{:S(2)}, u32[]{:S(2)}) %collective-permute-start.26) | collective-permute-done | bytes 1048608 | tf_op jit(solution)/shard_map/ppermute | solution.py:35
  359.3 4.7 convolution_select_fusion.2
  378.5 20.1 %collective-permute-done.16 = f32[4,512]{1,0:T(4,128)S(1)} collective-permute-done((f32[4,512]{1,0:T(4,128)S(1)}, f32[4,512]{1,0:T(4,128)S(1)}, u32[]{:S(2)}, u32[]{:S(2)}) %collective-permute-start.16) | collective-permute-done | bytes 8224 | tf_op jit(solution)/shard_map/ppermute | solution.py:35
  399.6 32.2 %collective-permute-start.17 = (f32[4,512]{1,0:T(4,128)S(1)}, f32[4,512]{1,0:T(4,128)S(1)}, u32[]{:S(2)}, u32[]{:S(2)}) collective-permute-start(f32[4,512]{1,0:T(4,128)S(1)} %fusion.24), channel_id=1, source_target_pairs={{2,0},{3,1},{4,2},{5,3},{6,4},{7,5},{8,6},{9,7},{10,8},{11,9},{12,... | collective-permute-start | bytes 24584 | tf_op jit(solution)/shard_map/ppermute | solution.py:35
  457.4 6.7 %collective-permute-done.23 = f32[4,512]{1,0:T(4,128)S(1)} collective-permute-done((f32[4,512]{1,0:T(4,128)S(1)}, f32[4,512]{1,0:T(4,128)S(1)}, u32[]{:S(2)}, u32[]{:S(2)}) %collective-permute-start.23) | collective-permute-done | bytes 8224 | tf_op jit(solution)/shard_map/ppermute | solution.py:35
  468.3 8.4 %collective-permute-done.25 = f32[4,512]{1,0:T(4,128)S(1)} collective-permute-done((f32[4,512]{1,0:T(4,128)S(1)}, f32[4,512]{1,0:T(4,128)S(1)}, u32[]{:S(2)}, u32[]{:S(2)}) %collective-permute-start.25) | collective-permute-done | bytes 8224 | tf_op jit(solution)/shard_map/ppermute | solution.py:35
  504.1 9.9 %all_to_all.15 = f32[2,4,4,512]{3,1,0,2:T(4,128)S(1)} all-to-all(f32[2,4,4,512]{3,1,0,2:T(4,128)S(1)} %copy.10), channel_id=1, replica_groups=mesh['tm'=64,'state'=4] {'state'}, dimensions={2} | all-to-all | bytes 131072 | tf_op jit(solution)/shard_map/all_to_all | solution.py:125
  (151 shorter events, 187.7 us)
Async XLA Ops:
  7.2 29.6 %all-gather.2.cloned.1.call-start = ((), (), s32[]{:S(2)}) async-start(), calls=%async_computation.1 | async-start | bytes 1310720 | tf_op jit(solution)/shard_map/all_gather | solution.py:51
  43.9 23.0 %collective-permute-start = (f32[512,512]{1,0:T(8,128)S(1)}, f32[512,512]{1,0:T(8,128)}, u32[]{:S(2)}, u32[]{:S(2)}) collective-permute-start(f32[512,512]{1,0:T(8,128)S(1)} %convolution_multiply_fusion.3), channel_id=1, source_target_pairs={{0,1},{1,2},{2,3},{3,4},{4,5},{5,6},{6,7},{7,8},{8,9},{9,10},{10,1... | collective-permute-start | bytes 3145736 | tf_op jit(solution)/shard_map/ppermute | solution.py:35
  70.1 29.1 %collective-permute-start.1 = (f32[512,512]{1,0:T(8,128)S(1)}, f32[512,512]{1,0:T(8,128)}, u32[]{:S(2)}, u32[]{:S(2)}) collective-permute-start(f32[512,512]{1,0:T(8,128)S(1)} %convolution_select_fusion.13), channel_id=1, source_target_pairs={{0,2},{1,3},{2,4},{3,5},{4,6},{5,7},{6,8},{7,9},{8,10},{9,11},{10,... | collective-permute-start | bytes 3145736 | tf_op jit(solution)/shard_map/ppermute | solution.py:35
  102.3 16.6 %collective-permute-start.2 = (f32[512,512]{1,0:T(8,128)S(1)}, f32[512,512]{1,0:T(8,128)S(1)}, u32[]{:S(2)}, u32[]{:S(2)}) collective-permute-start(f32[512,512]{1,0:T(8,128)S(1)} %convolution_select_fusion.12), channel_id=1, source_target_pairs={{0,4},{1,5},{2,6},{3,7},{4,8},{5,9},{6,10},{7,11},{8,12},{9,13},{1... | collective-permute-start | bytes 3145736 | tf_op jit(solution)/shard_map/ppermute | solution.py:35
  115.0 27.5 %collective-permute-start.18 = (f32[512,512]{1,0:T(8,128)S(1)}, f32[512,512]{1,0:T(8,128)}, u32[]{:S(2)}, u32[]{:S(2)}) collective-permute-start(f32[512,512]{1,0:T(8,128)S(1)} %fusion.5), channel_id=1, source_target_pairs={{1,0},{2,1},{3,2},{4,3},{5,4},{6,5},{7,6},{8,7},{9,8},{10,9},{11,1... | collective-permute-start | bytes 3145736 | tf_op jit(solution)/shard_map/ppermute | solution.py:35
  121.8 31.3 %collective-permute-start.3 = (f32[512,512]{1,0:T(8,128)}, f32[512,512]{1,0:T(8,128)}, u32[]{:S(2)}, u32[]{:S(2)}) collective-permute-start(f32[512,512]{1,0:T(8,128)} %convolution_select_fusion.11), channel_id=1, source_target_pairs={{0,8},{1,9},{2,10},{3,11},{4,12},{5,13},{6,14},{7,15},{8,16},{9,17... | collective-permute-start | bytes 3145736 | tf_op jit(solution)/shard_map/ppermute | solution.py:35
  145.5 29.5 %collective-permute-start.20 = (f32[512,512]{1,0:T(8,128)S(1)}, f32[512,512]{1,0:T(8,128)S(1)}, u32[]{:S(2)}, u32[]{:S(2)}) collective-permute-start(f32[512,512]{1,0:T(8,128)S(1)} %convolution_select_fusion.6), channel_id=1, source_target_pairs={{2,0},{3,1},{4,2},{5,3},{6,4},{7,5},{8,6},{9,7},{10,8},{11,9},{12,... | collective-permute-start | bytes 3145736 | tf_op jit(solution)/shard_map/ppermute | solution.py:35
  156.8 50.4 %collective-permute-start.4 = (f32[512,512]{1,0:T(8,128)S(1)}, f32[512,512]{1,0:T(8,128)S(1)}, u32[]{:S(2)}, u32[]{:S(2)}) collective-permute-start(f32[512,512]{1,0:T(8,128)S(1)} %convolution_select_fusion.10), channel_id=1, source_target_pairs={{0,16},{1,17},{2,18},{3,19},{4,20},{5,21},{6,22},{7,23},{8,24},{9,... | collective-permute-start | bytes 3145736 | tf_op jit(solution)/shard_map/ppermute | solution.py:35
  162.0 39.3 %collective-permute-start.7 = (f32[4,512]{1,0:T(4,128)S(1)}, f32[4,512]{1,0:T(4,128)S(1)}, u32[]{:S(2)}, u32[]{:S(2)}) collective-permute-start(f32[4,512]{1,0:T(4,128)S(1)} %fusion.46), channel_id=1, source_target_pairs={{0,1},{1,2},{2,3},{3,4},{4,5},{5,6},{6,7},{7,8},{8,9},{9,10},{10,1... | collective-permute-start | bytes 24584 | tf_op jit(solution)/shard_map/ppermute | solution.py:35
  177.9 59.8 %collective-permute-start.22 = (f32[512,512]{1,0:T(8,128)}, f32[512,512]{1,0:T(8,128)}, u32[]{:S(2)}, u32[]{:S(2)}) collective-permute-start(f32[512,512]{1,0:T(8,128)} %convolution_select_fusion.5), channel_id=1, source_target_pairs={{4,0},{5,1},{6,2},{7,3},{8,4},{9,5},{10,6},{11,7},{12,8},{13,9},{1... | collective-permute-start | bytes 3145736 | tf_op jit(solution)/shard_map/ppermute | solution.py:35
  202.3 17.1 %collective-permute-start.8 = (f32[4,512]{1,0:T(4,128)S(1)}, f32[4,512]{1,0:T(4,128)S(1)}, u32[]{:S(2)}, u32[]{:S(2)}) collective-permute-start(f32[4,512]{1,0:T(4,128)S(1)} %fusion.45), channel_id=1, source_target_pairs={{0,2},{1,3},{2,4},{3,5},{4,6},{5,7},{6,8},{7,9},{8,10},{9,11},{10,... | collective-permute-start | bytes 24584 | tf_op jit(solution)/shard_map/ppermute | solution.py:35
  210.0 70.9 %collective-permute-start.5 = (f32[512,512]{1,0:T(8,128)}, f32[512,512]{1,0:T(8,128)}, u32[]{:S(2)}, u32[]{:S(2)}) collective-permute-start(f32[512,512]{1,0:T(8,128)} %convolution_select_fusion.9), channel_id=1, source_target_pairs={{0,32},{1,33},{2,34},{3,35},{4,36},{5,37},{6,38},{7,39},{8,40},{9,... | collective-permute-start | bytes 3145736 | tf_op jit(solution)/shard_map/ppermute | solution.py:35
  220.4 13.0 %collective-permute-start.9 = (f32[4,512]{1,0:T(4,128)S(1)}, f32[4,512]{1,0:T(4,128)S(1)}, u32[]{:S(2)}, u32[]{:S(2)}) collective-permute-start(f32[4,512]{1,0:T(4,128)S(1)} %fusion.44), channel_id=1, source_target_pairs={{0,4},{1,5},{2,6},{3,7},{4,8},{5,9},{6,10},{7,11},{8,12},{9,13},{1... | collective-permute-start | bytes 24584 | tf_op jit(solution)/shard_map/ppermute | solution.py:35
  235.6 25.2 %collective-permute-start.10 = (f32[4,512]{1,0:T(4,128)S(1)}, f32[4,512]{1,0:T(4,128)S(1)}, u32[]{:S(2)}, u32[]{:S(2)}) collective-permute-start(f32[4,512]{1,0:T(4,128)S(1)} %fusion.43), channel_id=1, source_target_pairs={{0,8},{1,9},{2,10},{3,11},{4,12},{5,13},{6,14},{7,15},{8,16},{9,17... | collective-permute-start | bytes 24584 | tf_op jit(solution)/shard_map/ppermute | solution.py:35
  242.4 59.8 %collective-permute-start.24 = (f32[512,512]{1,0:T(8,128)}, f32[512,512]{1,0:T(8,128)}, u32[]{:S(2)}, u32[]{:S(2)}) collective-permute-start(f32[512,512]{1,0:T(8,128)} %convolution_select_fusion.4), channel_id=1, source_target_pairs={{8,0},{9,1},{10,2},{11,3},{12,4},{13,5},{14,6},{15,7},{16,8},{17,9... | collective-permute-start | bytes 3145736 | tf_op jit(solution)/shard_map/ppermute | solution.py:35
  263.0 24.6 %collective-permute-start.11 = (f32[4,512]{1,0:T(4,128)S(1)}, f32[4,512]{1,0:T(4,128)S(1)}, u32[]{:S(2)}, u32[]{:S(2)}) collective-permute-start(f32[4,512]{1,0:T(4,128)S(1)} %fusion.42), channel_id=1, source_target_pairs={{0,16},{1,17},{2,18},{3,19},{4,20},{5,21},{6,22},{7,23},{8,24},{9,... | collective-permute-start | bytes 24584 | tf_op jit(solution)/shard_map/ppermute | solution.py:35
  285.7 28.2 %collective-permute-start.6 = (f32[512,512]{1,0:T(8,128)}, f32[512,512]{1,0:T(8,128)}, u32[]{:S(2)}, u32[]{:S(2)}) collective-permute-start(f32[512,512]{1,0:T(8,128)} %convolution_select_fusion.8), channel_id=1, source_target_pairs={{0,64},{1,65},{2,66},{3,67},{4,68},{5,69},{6,70},{7,71},{8,72},{9,... | collective-permute-start | bytes 3145736 | tf_op jit(solution)/shard_map/ppermute | solution.py:35
  300.2 11.5 %collective-permute-start.13 = (f32[4,512]{1,0:T(4,128)S(1)}, f32[4,512]{1,0:T(4,128)S(1)}, u32[]{:S(2)}, u32[]{:S(2)}) collective-permute-start(f32[4,512]{1,0:T(4,128)S(1)} %fusion.40), channel_id=1, source_target_pairs={{0,64},{1,65},{2,66},{3,67},{4,68},{5,69},{6,70},{7,71},{8,72},{9,... | collective-permute-start | bytes 24584 | tf_op jit(solution)/shard_map/ppermute | solution.py:35
  306.8 52.4 %collective-permute-start.26 = (f32[512,512]{1,0:T(8,128)}, f32[512,512]{1,0:T(8,128)}, u32[]{:S(2)}, u32[]{:S(2)}) collective-permute-start(f32[512,512]{1,0:T(8,128)} %convolution_select_fusion.3), channel_id=1, source_target_pairs={{16,0},{17,1},{18,2},{19,3},{20,4},{21,5},{22,6},{23,7},{24,8},{25... | collective-permute-start | bytes 3145736 | tf_op jit(solution)/shard_map/ppermute | solution.py:35
  324.4 41.5 %collective-permute-start.15 = (f32[4,512]{1,0:T(4,128)S(1)}, f32[4,512]{1,0:T(4,128)S(1)}, u32[]{:S(2)}, u32[]{:S(2)}) collective-permute-start(f32[4,512]{1,0:T(4,128)S(1)} %fusion.38), channel_id=1, source_target_pairs={{0,1},{1,2},{2,3},{3,4},{4,5},{5,6},{6,7},{7,8},{8,9},{9,10},{10,1... | collective-permute-start | bytes 24584 | tf_op jit(solution)/shard_map/ppermute | solution.py:35
  364.0 73.5 %collective-permute-start.28 = (f32[512,512]{1,0:T(8,128)}, f32[512,512]{1,0:T(8,128)}, u32[]{:S(2)}, u32[]{:S(2)}) collective-permute-start(f32[512,512]{1,0:T(8,128)} %convolution_select_fusion.2), channel_id=1, source_target_pairs={{32,0},{33,1},{34,2},{35,3},{36,4},{37,5},{38,6},{39,7},{40,8},{41... | collective-permute-start | bytes 3145736 | tf_op jit(solution)/shard_map/ppermute | solution.py:35
  376.6 22.0 %collective-permute-start.16 = (f32[4,512]{1,0:T(4,128)S(1)}, f32[4,512]{1,0:T(4,128)S(1)}, u32[]{:S(2)}, u32[]{:S(2)}) collective-permute-start(f32[4,512]{1,0:T(4,128)S(1)} %fusion.26), channel_id=1, source_target_pairs={{1,0},{2,1},{3,2},{4,3},{5,4},{6,5},{7,6},{8,7},{9,8},{10,9},{11,1... | collective-permute-start | bytes 24584 | tf_op jit(solution)/shard_map/ppermute | solution.py:35
  399.6 33.6 %collective-permute-start.17 = (f32[4,512]{1,0:T(4,128)S(1)}, f32[4,512]{1,0:T(4,128)S(1)}, u32[]{:S(2)}, u32[]{:S(2)}) collective-permute-start(f32[4,512]{1,0:T(4,128)S(1)} %fusion.24), channel_id=1, source_target_pairs={{2,0},{3,1},{4,2},{5,3},{6,4},{7,5},{8,6},{9,7},{10,8},{11,9},{12,... | collective-permute-start | bytes 24584 | tf_op jit(solution)/shard_map/ppermute | solution.py:35
  441.2 45.5 %collective-permute-start.30 = (f32[512,512]{1,0:T(8,128)S(1)}, f32[512,512]{1,0:T(8,128)S(1)}, u32[]{:S(2)}, u32[]{:S(2)}) collective-permute-start(f32[512,512]{1,0:T(8,128)S(1)} %convolution_select_fusion.1), channel_id=1, source_target_pairs={{64,0},{65,1},{66,2},{67,3},{68,4},{69,5},{70,6},{71,7},{72,8},{73... | collective-permute-start | bytes 3145736 | tf_op jit(solution)/shard_map/ppermute | solution.py:35
  (23 other events, 392.6 us)
Sparse Core Ops, SparseCore 0:
  9.8 26.9 all-gather.1
where the time goes:
time: 532 us; the launch traced here: 523 us
  waiting for transfers between devices  234 us (44%)
  starting transfers between devices  143 us (27%)
  matrix products  111 us (21%)
  between operations  15.2 us (3%)
  blocking collectives  9.88 us (2%)
  local copies, waits for them, and re-layouts  6.3 us (1%)
    ppermute x32, waiting for transfers between devices, shifted(): return lax.ppermute(block, AXES, route)  206 us
    ppermute x32, starting transfers between devices, shifted(): return lax.ppermute(block, AXES, route)  143 us
    dot_general x26, matrix products, product(): jnp.dot(left, right, precision=lax.Precision.HIGHEST, preferred_element_t...  66.1 us
    dot_general x25, matrix products, transposed(): lax.dot_general(left, right, (((1,), (1,)), ((), ())), precision=lax.Prec...  35.1 us
    all_gather x1, waiting for transfers between devices, per_device(): lax.all_gather(dynamics, 'state', axis=0, tiled=True) * block_mask  27.4 us
  transfers between devices with their start and end apart: 33, of which 20 were waited for; matrix products, arithmetic and copies ran while one was open for 19% of the time, Pallas kernels for 0%

commit v1 on v0

--- a/solution.py
+++ b/solution.py
@@ -48,7 +48,12 @@
     steps_total = span * segments
     present = jnp.maximum(pattern, jnp.eye(blocks, dtype=jnp.int32))
     block_mask = jnp.repeat(jnp.repeat(present, block_span, 0), block_span, 1).astype(jnp.float32)
-    transition = lax.all_gather(dynamics, "state", axis=0, tiled=True) * block_mask
+    transition = (
+        jnp.concatenate(
+            lax.all_to_all(jnp.stack([dynamics] * lax.axis_size("state")), "state", 0, 0), axis=0
+        )
+        * block_mask
+    )
     first = member * span
     obs_here = lax.dynamic_slice_in_dim(observed, first, span, 0)
     index_here = lax.dynamic_slice_in_dim(obs_index, first, span, 0)

time: 532 us -> 514 us (0.966)
  the two profiles are of different devices: /device:TPU:232 before, /device:TPU:72 now
where the time goes in v1:
time: 514 us; the launch traced here: 504 us
  starting transfers between devices  186 us (36%)
  waiting for transfers between devices  179 us (35%)
  matrix products  112 us (22%)
  local copies, waits for them, and re-layouts  9.96 us (2%)
  blocking collectives  9.75 us (2%)
  other arithmetic  5.15 us (1%)
    ppermute x32, starting transfers between devices, shifted(): return lax.ppermute(block, AXES, route)  182 us
    ppermute x32, waiting for transfers between devices, shifted(): return lax.ppermute(block, AXES, route)  168 us
    dot_general x26, matrix products, product(): jnp.dot(left, right, precision=lax.Precision.HIGHEST, preferred_element_t...  66.9 us
    dot_general x25, matrix products, transposed(): lax.dot_general(left, right, (((1,), (1,)), ((), ())), precision=lax.Prec...  35.1 us
    all_to_all x1, waiting for transfers between devices, per_device(): lax.all_to_all(jnp.stack([dynamics] * lax.axis_size('state')), 'state', 0...  10.9 us
  transfers between devices with their start and end apart: 33, of which 18 were waited for; matrix products, arithmetic and copies ran while one was open for 20% of the time, Pallas kernels for 0%

profile of v1, /device:TPU:72, one launch (start us, length us, event | category | flops | bytes accessed | tf_op | source)
XLA Modules:
  0.0 503.9 jit_solution(7206248354455469568)
XLA Ops:
  11.2 10.9 %all-to-all-done = f32[4,128,512]{2,1,0:T(8,128)S(1)} async-done(((f32[4,128,512]{2,1,0:T(8,128)}), f32[4,128,512]{2,1,0:T(8,128)S(1)}, u32[]{:S(2)}, u32[]{:S(2)}) %all-to-all-start) | async-done | bytes 1048608 | tf_op jit(solution)/shard_map/all_to_all | solution.py:53
  32.3 21.2 %collective-permute-done = f32[512,512]{1,0:T(8,128)} collective-permute-done((f32[512,512]{1,0:T(8,128)S(1)}, f32[512,512]{1,0:T(8,128)}, u32[]{:S(2)}, u32[]{:S(2)}) %collective-permute-start) | collective-permute-done | bytes 1048608 | tf_op jit(solution)/shard_map/ppermute | solution.py:35
  57.3 4.8 collective-permute-start.1
  62.8 22.8 %collective-permute-done.1 = f32[512,512]{1,0:T(8,128)} collective-permute-done((f32[512,512]{1,0:T(8,128)S(1)}, f32[512,512]{1,0:T(8,128)}, u32[]{:S(2)}, u32[]{:S(2)}) %collective-permute-start.1) | collective-permute-done | bytes 1048608 | tf_op jit(solution)/shard_map/ppermute | solution.py:35
  92.2 4.8 fusion.2
  115.6 14.3 %collective-permute-done.18 = f32[512,512]{1,0:T(8,128)} collective-permute-done((f32[512,512]{1,0:T(8,128)S(1)}, f32[512,512]{1,0:T(8,128)}, u32[]{:S(2)}, u32[]{:S(2)}) %collective-permute-start.18) | collective-permute-done | bytes 1048608 | tf_op jit(solution)/shard_map/ppermute | solution.py:35
  133.0 4.7 collective-permute-start.20
  142.4 6.4 %collective-permute-start.4 = (f32[512,512]{1,0:T(8,128)S(1)}, f32[512,512]{1,0:T(8,128)S(1)}, u32[]{:S(2)}, u32[]{:S(2)}) collective-permute-start(f32[512,512]{1,0:T(8,128)S(1)} %convolution_select_fusion.10), channel_id=1, source_target_pairs={{0,16},{1,17},{2,18},{3,19},{4,20},{5,21},{6,22},{7,23},{8,24},{9,... | collective-permute-start | bytes 3145736 | tf_op jit(solution)/shard_map/ppermute | solution.py:35
  153.3 8.3 %collective-permute-done.20 = f32[512,512]{1,0:T(8,128)S(1)} collective-permute-done((f32[512,512]{1,0:T(8,128)S(1)}, f32[512,512]{1,0:T(8,128)S(1)}, u32[]{:S(2)}, u32[]{:S(2)}) %collective-permute-start.20) | collective-permute-done | bytes 1048608 | tf_op jit(solution)/shard_map/ppermute | solution.py:35
  166.4 27.6 %collective-permute-done.7 = f32[4,512]{1,0:T(4,128)S(1)} collective-permute-done((f32[4,512]{1,0:T(4,128)S(1)}, f32[4,512]{1,0:T(4,128)S(1)}, u32[]{:S(2)}, u32[]{:S(2)}) %collective-permute-start.7) | collective-permute-done | bytes 8224 | tf_op jit(solution)/shard_map/ppermute | solution.py:35
  212.7 22.1 %collective-permute-start.10 = (f32[4,512]{1,0:T(4,128)S(1)}, f32[4,512]{1,0:T(4,128)S(1)}, u32[]{:S(2)}, u32[]{:S(2)}) collective-permute-start(f32[4,512]{1,0:T(4,128)S(1)} %fusion.40), channel_id=1, source_target_pairs={{0,8},{1,9},{2,10},{3,11},{4,12},{5,13},{6,14},{7,15},{8,16},{9,17... | collective-permute-start | bytes 24584 | tf_op jit(solution)/shard_map/ppermute | solution.py:35
  234.8 4.7 convolution_select_fusion.4
  239.5 23.4 %collective-permute-start.24 = (f32[512,512]{1,0:T(8,128)}, f32[512,512]{1,0:T(8,128)}, u32[]{:S(2)}, u32[]{:S(2)}) collective-permute-start(f32[512,512]{1,0:T(8,128)} %convolution_select_fusion.4), channel_id=1, source_target_pairs={{8,0},{9,1},{10,2},{11,3},{12,4},{13,5},{14,6},{15,7},{16,8},{17,9... | collective-permute-start | bytes 3145736 | tf_op jit(solution)/shard_map/ppermute | solution.py:35
  268.0 4.8 convolution_select_fusion.8
  277.2 5.3 %collective-permute-start.12 = (f32[4,512]{1,0:T(4,128)S(1)}, f32[4,512]{1,0:T(4,128)S(1)}, u32[]{:S(2)}, u32[]{:S(2)}) collective-permute-start(f32[4,512]{1,0:T(4,128)S(1)} %fusion.38), channel_id=1, source_target_pairs={{0,32},{1,33},{2,34},{3,35},{4,36},{5,37},{6,38},{7,39},{8,40},{9,... | collective-permute-start | bytes 24584 | tf_op jit(solution)/shard_map/ppermute | solution.py:35
  282.6 5.1 %collective-permute-done.12 = f32[4,512]{1,0:T(4,128)S(1)} collective-permute-done((f32[4,512]{1,0:T(4,128)S(1)}, f32[4,512]{1,0:T(4,128)S(1)}, u32[]{:S(2)}, u32[]{:S(2)}) %collective-permute-start.12) | collective-permute-done | bytes 8224 | tf_op jit(solution)/shard_map/ppermute | solution.py:35
  291.8 4.7 convolution_select_fusion.3
  317.1 28.6 %collective-permute-done.26 = f32[512,512]{1,0:T(8,128)} collective-permute-done((f32[512,512]{1,0:T(8,128)}, f32[512,512]{1,0:T(8,128)}, u32[]{:S(2)}, u32[]{:S(2)}) %collective-permute-start.26) | collective-permute-done | bytes 1048608 | tf_op jit(solution)/shard_map/ppermute | solution.py:35
  345.8 4.8 convolution_select_fusion.2
  350.5 52.2 %collective-permute-start.28 = (f32[512,512]{1,0:T(8,128)}, f32[512,512]{1,0:T(8,128)}, u32[]{:S(2)}, u32[]{:S(2)}) collective-permute-start(f32[512,512]{1,0:T(8,128)} %convolution_select_fusion.2), channel_id=1, source_target_pairs={{32,0},{33,1},{34,2},{35,3},{36,4},{37,5},{38,6},{39,7},{40,8},{41... | collective-permute-start | bytes 3145736 | tf_op jit(solution)/shard_map/ppermute | solution.py:35
  421.8 5.1 %collective-permute-done.17 = f32[4,512]{1,0:T(4,128)S(1)} collective-permute-done((f32[4,512]{1,0:T(4,128)S(1)}, f32[4,512]{1,0:T(4,128)S(1)}, u32[]{:S(2)}, u32[]{:S(2)}) %collective-permute-start.17) | collective-permute-done | bytes 8224 | tf_op jit(solution)/shard_map/ppermute | solution.py:35
  447.6 5.7 %collective-permute-done.23 = f32[4,512]{1,0:T(4,128)S(1)} collective-permute-done((f32[4,512]{1,0:T(4,128)S(1)}, f32[4,512]{1,0:T(4,128)S(1)}, u32[]{:S(2)}, u32[]{:S(2)}) %collective-permute-start.23) | collective-permute-done | bytes 8224 | tf_op jit(solution)/shard_map/ppermute | solution.py:35
  459.4 5.6 %collective-permute-done.25 = f32[4,512]{1,0:T(4,128)S(1)} collective-permute-done((f32[4,512]{1,0:T(4,128)S(1)}, f32[4,512]{1,0:T(4,128)S(1)}, u32[]{:S(2)}, u32[]{:S(2)}) %collective-permute-start.25) | collective-permute-done | bytes 8224 | tf_op jit(solution)/shard_map/ppermute | solution.py:35
  492.4 9.8 %all_to_all.20 = f32[2,4,4,512]{3,1,0,2:T(4,128)S(1)} all-to-all(f32[2,4,4,512]{3,1,0,2:T(4,128)S(1)} %copy.10), channel_id=1, replica_groups=mesh['tm'=64,'state'=4] {'state'}, dimensions={2} | all-to-all | bytes 131072 | tf_op jit(solution)/shard_map/all_to_all | solution.py:130
  (156 shorter events, 194.1 us)
Async XLA Ops:
  2.7 19.4 %all-to-all-start = ((f32[4,128,512]{2,1,0:T(8,128)}), f32[4,128,512]{2,1,0:T(8,128)S(1)}, u32[]{:S(2)}, u32[]{:S(2)}) async-start(f32[4,128,512]{2,1,0:T(8,128)} %stack.46), calls=%async_computation | async-start | bytes 2097152 | tf_op jit(solution)/shard_map/all_to_all | solution.py:53
  29.8 23.7 %collective-permute-start = (f32[512,512]{1,0:T(8,128)S(1)}, f32[512,512]{1,0:T(8,128)}, u32[]{:S(2)}, u32[]{:S(2)}) collective-permute-start(f32[512,512]{1,0:T(8,128)S(1)} %convolution_multiply_fusion.3), channel_id=1, source_target_pairs={{0,1},{1,2},{2,3},{3,4},{4,5},{5,6},{6,7},{7,8},{8,9},{9,10},{10,1... | collective-permute-start | bytes 3145736 | tf_op jit(solution)/shard_map/ppermute | solution.py:35
  57.3 28.3 %collective-permute-start.1 = (f32[512,512]{1,0:T(8,128)S(1)}, f32[512,512]{1,0:T(8,128)}, u32[]{:S(2)}, u32[]{:S(2)}) collective-permute-start(f32[512,512]{1,0:T(8,128)S(1)} %convolution_select_fusion.13), channel_id=1, source_target_pairs={{0,2},{1,3},{2,4},{3,5},{4,6},{5,7},{6,8},{7,9},{8,10},{9,11},{10,... | collective-permute-start | bytes 3145736 | tf_op jit(solution)/shard_map/ppermute | solution.py:35
  88.7 17.2 %collective-permute-start.2 = (f32[512,512]{1,0:T(8,128)S(1)}, f32[512,512]{1,0:T(8,128)S(1)}, u32[]{:S(2)}, u32[]{:S(2)}) collective-permute-start(f32[512,512]{1,0:T(8,128)S(1)} %convolution_select_fusion.12), channel_id=1, source_target_pairs={{0,4},{1,5},{2,6},{3,7},{4,8},{5,9},{6,10},{7,11},{8,12},{9,13},{1... | collective-permute-start | bytes 3145736 | tf_op jit(solution)/shard_map/ppermute | solution.py:35
  102.2 27.7 %collective-permute-start.18 = (f32[512,512]{1,0:T(8,128)S(1)}, f32[512,512]{1,0:T(8,128)}, u32[]{:S(2)}, u32[]{:S(2)}) collective-permute-start(f32[512,512]{1,0:T(8,128)S(1)} %fusion), channel_id=1, source_target_pairs={{1,0},{2,1},{3,2},{4,3},{5,4},{6,5},{7,6},{8,7},{9,8},{10,9},{11,1... | collective-permute-start | bytes 3145736 | tf_op jit(solution)/shard_map/ppermute | solution.py:35
  108.8 29.9 %collective-permute-start.3 = (f32[512,512]{1,0:T(8,128)}, f32[512,512]{1,0:T(8,128)}, u32[]{:S(2)}, u32[]{:S(2)}) collective-permute-start(f32[512,512]{1,0:T(8,128)} %convolution_select_fusion.11), channel_id=1, source_target_pairs={{0,8},{1,9},{2,10},{3,11},{4,12},{5,13},{6,14},{7,15},{8,16},{9,17... | collective-permute-start | bytes 3145736 | tf_op jit(solution)/shard_map/ppermute | solution.py:35
  133.0 28.6 %collective-permute-start.20 = (f32[512,512]{1,0:T(8,128)S(1)}, f32[512,512]{1,0:T(8,128)S(1)}, u32[]{:S(2)}, u32[]{:S(2)}) collective-permute-start(f32[512,512]{1,0:T(8,128)S(1)} %convolution_select_fusion.6), channel_id=1, source_target_pairs={{2,0},{3,1},{4,2},{5,3},{6,4},{7,5},{8,6},{9,7},{10,8},{11,9},{12,... | collective-permute-start | bytes 3145736 | tf_op jit(solution)/shard_map/ppermute | solution.py:35
  142.4 54.6 %collective-permute-start.4 = (f32[512,512]{1,0:T(8,128)S(1)}, f32[512,512]{1,0:T(8,128)S(1)}, u32[]{:S(2)}, u32[]{:S(2)}) collective-permute-start(f32[512,512]{1,0:T(8,128)S(1)} %convolution_select_fusion.10), channel_id=1, source_target_pairs={{0,16},{1,17},{2,18},{3,19},{4,20},{5,21},{6,22},{7,23},{8,24},{9,... | collective-permute-start | bytes 3145736 | tf_op jit(solution)/shard_map/ppermute | solution.py:35
  150.8 43.2 %collective-permute-start.7 = (f32[4,512]{1,0:T(4,128)S(1)}, f32[4,512]{1,0:T(4,128)S(1)}, u32[]{:S(2)}, u32[]{:S(2)}) collective-permute-start(f32[4,512]{1,0:T(4,128)S(1)} %fusion.43), channel_id=1, source_target_pairs={{0,1},{1,2},{2,3},{3,4},{4,5},{5,6},{6,7},{7,8},{8,9},{9,10},{10,1... | collective-permute-start | bytes 24584 | tf_op jit(solution)/shard_map/ppermute | solution.py:35
  164.5 70.4 %collective-permute-start.22 = (f32[512,512]{1,0:T(8,128)}, f32[512,512]{1,0:T(8,128)}, u32[]{:S(2)}, u32[]{:S(2)}) collective-permute-start(f32[512,512]{1,0:T(8,128)} %convolution_select_fusion.5), channel_id=1, source_target_pairs={{4,0},{5,1},{6,2},{7,3},{8,4},{9,5},{10,6},{11,7},{12,8},{13,9},{1... | collective-permute-start | bytes 3145736 | tf_op jit(solution)/shard_map/ppermute | solution.py:35
  195.0 8.8 %collective-permute-start.8 = (f32[4,512]{1,0:T(4,128)S(1)}, f32[4,512]{1,0:T(4,128)S(1)}, u32[]{:S(2)}, u32[]{:S(2)}) collective-permute-start(f32[4,512]{1,0:T(4,128)S(1)} %fusion.42), channel_id=1, source_target_pairs={{0,2},{1,3},{2,4},{3,5},{4,6},{5,7},{6,8},{7,9},{8,10},{9,11},{10,... | collective-permute-start | bytes 24584 | tf_op jit(solution)/shard_map/ppermute | solution.py:35
  200.0 68.0 %collective-permute-start.5 = (f32[512,512]{1,0:T(8,128)}, f32[512,512]{1,0:T(8,128)}, u32[]{:S(2)}, u32[]{:S(2)}) collective-permute-start(f32[512,512]{1,0:T(8,128)} %convolution_select_fusion.9), channel_id=1, source_target_pairs={{0,32},{1,33},{2,34},{3,35},{4,36},{5,37},{6,38},{7,39},{8,40},{9,... | collective-permute-start | bytes 3145736 | tf_op jit(solution)/shard_map/ppermute | solution.py:35
  212.7 50.2 %collective-permute-start.10 = (f32[4,512]{1,0:T(4,128)S(1)}, f32[4,512]{1,0:T(4,128)S(1)}, u32[]{:S(2)}, u32[]{:S(2)}) collective-permute-start(f32[4,512]{1,0:T(4,128)S(1)} %fusion.40), channel_id=1, source_target_pairs={{0,8},{1,9},{2,10},{3,11},{4,12},{5,13},{6,14},{7,15},{8,16},{9,17... | collective-permute-start | bytes 24584 | tf_op jit(solution)/shard_map/ppermute | solution.py:35
  239.5 52.3 %collective-permute-start.24 = (f32[512,512]{1,0:T(8,128)}, f32[512,512]{1,0:T(8,128)}, u32[]{:S(2)}, u32[]{:S(2)}) collective-permute-start(f32[512,512]{1,0:T(8,128)} %convolution_select_fusion.4), channel_id=1, source_target_pairs={{8,0},{9,1},{10,2},{11,3},{12,4},{13,5},{14,6},{15,7},{16,8},{17,9... | collective-permute-start | bytes 3145736 | tf_op jit(solution)/shard_map/ppermute | solution.py:35
  265.1 11.1 %collective-permute-start.11 = (f32[4,512]{1,0:T(4,128)S(1)}, f32[4,512]{1,0:T(4,128)S(1)}, u32[]{:S(2)}, u32[]{:S(2)}) collective-permute-start(f32[4,512]{1,0:T(4,128)S(1)} %fusion.39), channel_id=1, source_target_pairs={{0,16},{1,17},{2,18},{3,19},{4,20},{5,21},{6,22},{7,23},{8,24},{9,... | collective-permute-start | bytes 24584 | tf_op jit(solution)/shard_map/ppermute | solution.py:35
  272.8 29.7 %collective-permute-start.6 = (f32[512,512]{1,0:T(8,128)}, f32[512,512]{1,0:T(8,128)}, u32[]{:S(2)}, u32[]{:S(2)}) collective-permute-start(f32[512,512]{1,0:T(8,128)} %convolution_select_fusion.8), channel_id=1, source_target_pairs={{0,64},{1,65},{2,66},{3,67},{4,68},{5,69},{6,70},{7,71},{8,72},{9,... | collective-permute-start | bytes 3145736 | tf_op jit(solution)/shard_map/ppermute | solution.py:35
  277.2 10.5 %collective-permute-start.12 = (f32[4,512]{1,0:T(4,128)S(1)}, f32[4,512]{1,0:T(4,128)S(1)}, u32[]{:S(2)}, u32[]{:S(2)}) collective-permute-start(f32[4,512]{1,0:T(4,128)S(1)} %fusion.38), channel_id=1, source_target_pairs={{0,32},{1,33},{2,34},{3,35},{4,36},{5,37},{6,38},{7,39},{8,40},{9,... | collective-permute-start | bytes 24584 | tf_op jit(solution)/shard_map/ppermute | solution.py:35
  289.8 10.5 %collective-permute-start.13 = (f32[4,512]{1,0:T(4,128)S(1)}, f32[4,512]{1,0:T(4,128)S(1)}, u32[]{:S(2)}, u32[]{:S(2)}) collective-permute-start(f32[4,512]{1,0:T(4,128)S(1)} %fusion.37), channel_id=1, source_target_pairs={{0,64},{1,65},{2,66},{3,67},{4,68},{5,69},{6,70},{7,71},{8,72},{9,... | collective-permute-start | bytes 24584 | tf_op jit(solution)/shard_map/ppermute | solution.py:35
  296.5 49.3 %collective-permute-start.26 = (f32[512,512]{1,0:T(8,128)}, f32[512,512]{1,0:T(8,128)}, u32[]{:S(2)}, u32[]{:S(2)}) collective-permute-start(f32[512,512]{1,0:T(8,128)} %convolution_select_fusion.3), channel_id=1, source_target_pairs={{16,0},{17,1},{18,2},{19,3},{20,4},{21,5},{22,6},{23,7},{24,8},{25... | collective-permute-start | bytes 3145736 | tf_op jit(solution)/shard_map/ppermute | solution.py:35
  315.0 87.7 %collective-permute-start.15 = (f32[4,512]{1,0:T(4,128)S(1)}, f32[4,512]{1,0:T(4,128)S(1)}, u32[]{:S(2)}, u32[]{:S(2)}) collective-permute-start(f32[4,512]{1,0:T(4,128)S(1)} %fusion.35), channel_id=1, source_target_pairs={{0,1},{1,2},{2,3},{3,4},{4,5},{5,6},{6,7},{7,8},{8,9},{9,10},{10,1... | collective-permute-start | bytes 24584 | tf_op jit(solution)/shard_map/ppermute | solution.py:35
  350.5 79.3 %collective-permute-start.28 = (f32[512,512]{1,0:T(8,128)}, f32[512,512]{1,0:T(8,128)}, u32[]{:S(2)}, u32[]{:S(2)}) collective-permute-start(f32[512,512]{1,0:T(8,128)} %convolution_select_fusion.2), channel_id=1, source_target_pairs={{32,0},{33,1},{34,2},{35,3},{36,4},{37,5},{38,6},{39,7},{40,8},{41... | collective-permute-start | bytes 3145736 | tf_op jit(solution)/shard_map/ppermute | solution.py:35
  427.9 7.9 %collective-permute-start.19 = (f32[4,512]{1,0:T(4,128)S(1)}, f32[4,512]{1,0:T(4,128)S(1)}, u32[]{:S(2)}, u32[]{:S(2)}) collective-permute-start(f32[4,512]{1,0:T(4,128)S(1)} %fusion.20), channel_id=1, source_target_pairs={{4,0},{5,1},{6,2},{7,3},{8,4},{9,5},{10,6},{11,7},{12,8},{13,9},{1... | collective-permute-start | bytes 24584 | tf_op jit(solution)/shard_map/ppermute | solution.py:35
  433.6 41.4 %collective-permute-start.30 = (f32[512,512]{1,0:T(8,128)S(1)}, f32[512,512]{1,0:T(8,128)S(1)}, u32[]{:S(2)}, u32[]{:S(2)}) collective-permute-start(f32[512,512]{1,0:T(8,128)S(1)} %convolution_select_fusion.1), channel_id=1, source_target_pairs={{64,0},{65,1},{66,2},{67,3},{68,4},{69,5},{70,6},{71,7},{72,8},{73... | collective-permute-start | bytes 3145736 | tf_op jit(solution)/shard_map/ppermute | solution.py:35
  455.6 9.5 %collective-permute-start.25 = (f32[4,512]{1,0:T(4,128)S(1)}, f32[4,512]{1,0:T(4,128)S(1)}, u32[]{:S(2)}, u32[]{:S(2)}) collective-permute-start(f32[4,512]{1,0:T(4,128)S(1)} %fusion.17), channel_id=1, source_target_pairs={{32,0},{33,1},{34,2},{35,3},{36,4},{37,5},{38,6},{39,7},{40,8},{41... | collective-permute-start | bytes 24584 | tf_op jit(solution)/shard_map/ppermute | solution.py:35
  (26 other events, 382.8 us)
